TPU v7x, 32 devices: a whole 2x2x4 slice. The times are simulated.
32 devices in a mesh: seq: 4 (over z), ch: 8 (over y, x, core).
Axes of the slice: x: 2, y: 2, z: 4, core: 2. Of those that a mesh axis runs over, the one named last changes fastest.
Arguments:
- inputs: bfloat16 [1024, 8192], P('seq', 'ch'), may hold values from -6 to 6
- w_in: bfloat16 [3, 8192, 8192], P(None, 'seq', 'ch'), may hold values from -0.0625 to 0.0625
- short_filter: float32 [3, 3, 8192], P(None, None, 'ch'), may hold values from -3 to 3
- rates: float32 [16, 8192], P(None, 'ch'), may hold values from 9.765625e-05 to 0.05
- residues: float32 [16, 8192], P(None, 'ch'), may hold values from -3 to 3
- skip: float32 [8192], P('ch'), may hold values from -3 to 3
Outputs:
- gated: bfloat16 [1024, 8192], P('seq', 'ch')
All inputs are finite; a program needn't handle non-finite values.
Results may differ from a plain program's by a relative error of at most 0.0065.
Values may be sent and summed in bfloat16 or wider, within the bound.
No kernel may reach another device: no remote copies, remote signals or barrier semaphores. Data moves between devices by JAX's collectives and lax.ppermute only.
A program may use at most 128 MiB of HBM per device.

v0:
```python
import jax
import jax.numpy as jnp
from jax import lax
from jax.sharding import PartitionSpec as P

TAPS = 3


def passed_along(block, axis, distance):
    devices = range(lax.axis_size(axis))
    route = [(i - distance, i) for i in devices if i - distance in devices]
    return lax.ppermute(block, axis, route)


def carried_in(part, axis, combine, identity):
    place = lax.axis_index(axis)
    gathered = jax.tree.map(lambda a: lax.all_gather(a, axis), part)
    state = jax.tree.map(lambda a, e: jnp.zeros_like(a) + jnp.asarray(e, a.dtype), part, identity)

    def one(hop, state):
        return combine(
            state, jax.tree.map(lambda a: lax.dynamic_index_in_dim(a, hop, 0, False), gathered)
        )

    return lax.fori_loop(0, place, one, state)


def combine(earlier, later):
    return (earlier[0] * later[0], earlier[1] * later[0] + later[1])


def project(inputs, w_in):
    tok_rows = inputs.shape[0]
    n_seq = lax.axis_size("seq")
    n_ch = lax.axis_size("ch")
    features = lax.all_gather(inputs, "ch", axis=1, tiled=True)
    piece = features.shape[1] // (n_seq * n_ch)
    features = features.reshape(tok_rows, n_seq, n_ch, piece)
    mine = lax.dynamic_index_in_dim(features, lax.axis_index("ch"), 2, False)
    rows = lax.all_to_all(mine, "seq", 1, 0, tiled=True)
    rows = rows.reshape(n_seq * tok_rows, piece)
    block = lax.all_gather(rows, "ch", axis=1, tiled=True)
    partial = jnp.einsum("td,kdc->ktc", block, w_in, preferred_element_type=jnp.float32)
    return lax.psum_scatter(partial, "seq", scatter_dimension=1, tiled=True)


def per_device(inputs, w_in, short_filter, rates, residues, skip):
    tok_rows = inputs.shape[0]
    width = w_in.shape[2]
    modes = rates.shape[0]
    proj = project(inputs, w_in).astype(jnp.bfloat16)
    prior = passed_along(proj[:, tok_rows - (TAPS - 1) :, :], "seq", 1)
    padded = jnp.concatenate([prior, proj], axis=1).astype(jnp.float32)
    mixed = jnp.zeros((3, tok_rows, width), jnp.float32)
    for j in range(TAPS):
        mixed = (
            mixed
            + short_filter[:, j, None, :] * padded[:, TAPS - 1 - j : TAPS - 1 - j + tok_rows, :]
        )
    query, key, value = (mixed[0], mixed[1], mixed[2])
    drive = key * value
    position = jnp.arange(tok_rows, dtype=jnp.float32)
    scaled = residues * jnp.sqrt(1.0 - jnp.exp(-2.0 * rates))
    end_powers = jnp.exp(-rates[None, :, :] * (tok_rows - 1.0 - position)[:, None, None])
    end_state = jnp.sum(end_powers * drive[:, None, :], axis=0)
    block_decay = jnp.exp(-rates * tok_rows)
    identity = (jnp.ones_like(block_decay), jnp.zeros_like(end_state))
    entering = carried_in((block_decay, end_state), "seq", combine, identity)[1]
    start_powers = jnp.exp(-rates[None, :, :] * (position + 1.0)[:, None, None])
    cross = jnp.sum(start_powers * (scaled * entering)[None, :, :], axis=1)
    center = (tok_rows - 1.0) / 2.0
    offset = (position - center)[:, None, None]
    rising = jnp.exp(rates[None, :, :] * offset) * drive[:, None, :]
    offsets = jnp.arange(tok_rows, dtype=jnp.int32)
    lower = (offsets[:, None] >= offsets[None, :]).astype(jnp.float32)
    prefix = jnp.dot(
        lower, rising.reshape(tok_rows, modes * width), precision=lax.Precision.HIGHEST
    )
    prefix = prefix.reshape(tok_rows, modes, width)
    falling = jnp.exp(-rates[None, :, :] * offset) * scaled[None, :, :]
    local = jnp.sum(falling * prefix, axis=1)
    return (query * (local + cross + skip[None, :] * drive)).astype(jnp.bfloat16)


def solution(mesh):
    in_specs = (
        P("seq", "ch"),
        P(None, "seq", "ch"),
        P(None, None, "ch"),
        P(None, "ch"),
        P(None, "ch"),
        P("ch"),
    )
    out_specs = P("seq", "ch")
    return jax.shard_map(
        per_device, mesh=mesh, in_specs=in_specs, out_specs=out_specs, check_vma=False
    )
```

profile of v0, /device:TPU:26, one launch (start us, length us, event | category | flops | bytes accessed | tf_op | source)
XLA Modules:
  0.0 415.0 jit_solution(5616361309072354084)
XLA Ops:
  6.5 0.0 all-gather.5.cloned.1.call-start
  6.5 0.7 all-gather.5.cloned.1.call-update
  7.3 0.0 all-gather.7.cloned.1.call-start
  7.3 39.5 %all-gather.5.cloned.1.call-done = bf16[256,8192]{1,0:T(8,128)(2,1)} async-done(((bf16[256,1024]{1,0:T(8,128)(2,1)}), bf16[256,8192]{1,0:T(8,128)(2,1)}) %all-gather.5.cloned.1.call-update) | async-done | bytes 4194320 | tf_op jit(solution)/shard_map/all_gather | solution.py:36
  46.8 3.6 copy.15
  50.4 1.1 constant_dynamic-slice_fusion
  51.5 0.2 copy.21
  51.7 17.5 %all_to_all.15 = bf16[256,4,256]{2,0,1:T(8,128)(2,1)} all-to-all(bf16[256,4,256]{2,0,1:T(8,128)(2,1)S(1)} %bitcast.60), channel_id=1, replica_groups=mesh['seq'=4,'ch'=8] {'seq'}, dimensions={1} | all-to-all | bytes 1048576 | tf_op jit(solution)/shard_map/all_to_all | solution.py:40
  69.2 0.0 all-gather.7.cloned.1.call-update
  69.2 0.0 reduce-scatter.2.cloned.1.call-start
  69.3 37.4 %all-gather.7.cloned.1.call-done = bf16[1024,2048]{1,0:T(8,128)(2,1)} async-done(((bf16[1024,256]{1,0:T(8,128)(2,1)}), bf16[1024,2048]{1,0:T(8,128)(2,1)}) %all-gather.7.cloned.1.call-update) | async-done | bytes 4194320 | tf_op jit(solution)/shard_map/all_gather | solution.py:42
  106.7 18.9 %convolution_bitcast_fusion = f32[3,1024,1024]{2,1,0:T(8,128)} fusion(bf16[3,2048,1024]{2,1,0:T(8,128)(2,1)} %param.9, bf16[1024,2048]{1,0:T(8,128)(2,1)} %all-gather.7.cloned.1.call-done), kind=kOutput, calls=%fused_computation.6 | convolution fusion | flops 12884901888 | bytes 29360128 | tf_op jit(solution)/shard_map/td,kdc->ktc/dot_general | solution.py:43
  125.6 0.0 copy-start.2
  125.6 0.0 copy-start
  125.6 0.0 reduce-scatter.2.cloned.1.call-update
  125.7 0.7 copy-done.2
  126.5 0.0 copy-done
  126.5 0.6 fusion.9
  127.1 210.6 %reduce-scatter.2.cloned.1.call-done = f32[3,256,1024]{2,1,0:T(8,128)} async-done(((f32[3,1024,1024]{2,1,0:T(8,128)}), f32[3,256,1024]{2,1,0:T(8,128)}) %reduce-scatter.2.cloned.1.call-update) | async-done | bytes 3145744 | tf_op jit(solution)/shard_map/reduce_scatter | solution.py:44
  337.7 2.1 convert_element_type.10
  339.9 1.3 collective-permute-start
  341.2 15.8 %all-gather = f32[64,1024]{1,0:T(8,128)S(1)} all-gather(f32[16,1024]{1,0:T(8,128)S(1)} %get-tuple-element.63), channel_id=2, replica_groups=mesh['seq'=4,'ch'=8] {'seq'}, dimensions={0}, use_global_device_ids=true | all-gather | bytes 327680 | tf_op jit(solution)/shard_map/all_gather | solution.py:17
  357.0 0.6 copy.16
  357.6 0.0 collective-permute-done
  357.6 0.5 maximum_convert_fusion
  358.1 0.9 fusion.1
  359.0 1.2 fusion.3
  360.2 2.5 copy.14
  362.7 4.1 multiply_reduce_fusion.1
  366.8 14.6 %all-gather.1 = f32[64,1024]{1,0:T(8,128)} all-gather(f32[16,1024]{1,0:T(8,128)S(1)} %multiply_reduce_fusion.1), channel_id=3, replica_groups=mesh['seq'=4,'ch'=8] {'seq'}, dimensions={0}, use_global_device_ids=true | all-gather | bytes 327680 | tf_op jit(solution)/shard_map/all_gather | solution.py:17
  381.4 2.9 while.12
  381.4 0.9 bitcast_add_fusion.2
  382.3 0.9 bitcast_add_fusion.2
  383.2 0.9 bitcast_add_fusion.2
  384.3 0.0 copy-start.1
  384.3 0.9 fusion.8
  385.2 3.9 bitcast_multiply_fusion.1
  389.1 0.0 copy-done.1
  389.1 0.0 copy-start.3
  389.2 13.9 %multiply_reduce_fusion.2 = f32[256,1024]{1,0:T(8,128)} fusion(f32[16,1024,256]{2,1,0:T(8,128)S(1)} %bitcast.57, f32[16,1024]{1,0:T(8,128)S(1)} %get-tuple-element.61, f32[256]{0:T(256)S(1)} %iota_add_fusion.1, f32[16,1024]{1,0:T(8,128)S(1)} %copy-done.1), kind=kOutput, calls=%fused_computation.5 | convolution fusion | flops 12901482496 | bytes 17957888 | tf_op jit(solution)/shard_map/dot_general | solution.py:76
  403.1 2.8 multiply_reduce_fusion
  405.9 0.0 copy-done.3
  405.9 2.6 fusion.5
  (8 shorter events, 0.1 us)
Async XLA Ops:
  6.5 40.3 %all-gather.5.cloned.1.call-start = ((), (), s32[]{:S(2)}) async-start(), calls=%async_computation.2 | async-start | bytes 4718592 | tf_op jit(solution)/shard_map/all_gather | solution.py:36
  7.3 99.5 %all-gather.7.cloned.1.call-start = ((), (), s32[]{:S(2)}) async-start(), calls=%async_computation.3 | async-start | bytes 4718592 | tf_op jit(solution)/shard_map/all_gather | solution.py:42
  69.2 268.5 %reduce-scatter.2.cloned.1.call-start = ((), (), s32[]{:S(2)}) async-start(), calls=%async_computation.4 | async-start | bytes 15728640 | tf_op jit(solution)/shard_map/reduce_scatter | solution.py:44
  125.6 0.8 copy-start.2
  125.6 0.9 copy-start
  339.9 17.7 %collective-permute-start = (bf16[3,2,1024]{2,1,0:T(2,128)(2,1)S(1)}, bf16[3,2,1024]{2,1,0:T(2,128)(2,1)S(1)}, u32[]{:S(2)}, u32[]{:S(2)}) collective-permute-start(bf16[3,2,1024]{2,1,0:T(2,128)(2,1)S(1)} %slice.40), channel_id=1, source_target_pairs={{0,8},{8,16},{16,24},{1,9},{9,17},{17,25},{2,10},{10,18},{18,26},{... | collective-permute-start | bytes 36872 | tf_op jit(solution)/shard_map/ppermute | solution.py:12
  384.3 4.8 %copy-start.1 = (f32[16,1024]{1,0:T(8,128)S(1)}, f32[16,1024]{1,0:T(8,128)}, u32[]{:S(2)}) copy-start(f32[16,1024]{1,0:T(8,128)} %get-tuple-element.62) | copy-start | bytes 196612
  389.1 16.7 %copy-start.3 = (f32[1024]{0:T(1024)S(1)}, f32[1024]{0:T(1024)}, u32[]{:S(2)}) copy-start(f32[1024]{0:T(1024)} %param.13) | copy-start | bytes 12292
Sparse Core Ops, SparseCore 0:
  9.2 37.5 all-gather.4
  69.3 37.3 all-gather.6
  125.8 211.8 reduce-scatter.1
where the time goes:
time: 416 us; the launch traced here: 415 us
  waiting for transfers between devices  288 us (69%)
  blocking collectives  47.9 us (12%)
  matrix products  32.8 us (8%)
  other arithmetic  22.3 us (5%)
  between operations  13.3 us (3%)
  local copies, waits for them, and re-layouts  8.82 us (2%)
    reduce_scatter x1, waiting for transfers between devices, project(): return lax.psum_scatter(partial, 'seq', scatter_dimension=1, tiled=True)  211 us
    all_gather x1, waiting for transfers between devices, project(): features = lax.all_gather(inputs, 'ch', axis=1, tiled=True)  39.5 us
    all_gather x1, waiting for transfers between devices, project(): block = lax.all_gather(rows, 'ch', axis=1, tiled=True)  37.4 us
    all_gather x2, blocking collectives, carried_in(): gathered = jax.tree.map(lambda a: lax.all_gather(a, axis), part)  30.4 us
    dot_general x1, matrix products, project(): jnp.einsum('td,kdc->ktc', block, w_in, preferred_element_type=jnp.float32)  18.9 us
    all_to_all x1, blocking collectives, project(): rows = lax.all_to_all(mine, 'seq', 1, 0, tiled=True)  17.5 us
    dot_general x1, matrix products, per_device(): jnp.dot(lower, rising.reshape(tok_rows, modes * width), precision=lax.Pre...  13.9 us
  transfers between devices with their start and end apart: 4, of which 3 were waited for; matrix products, arithmetic and copies ran while one was open for 0% of the time, Pallas kernels for 0%

commit v1 on v0

--- a/solution.py
+++ b/solution.py
@@ -4,6 +4,18 @@
 from jax.sharding import PartitionSpec as P
 
 TAPS = 3
+
+
+def summed_around(value, axis, dim, contribution):
+    size, mine, rows = (lax.axis_size(axis), lax.axis_index(axis), value.shape[dim])
+    right = [(i, (i + 1) % size) for i in range(size)]
+    block, total = (value, None)
+    for turn in range(size):
+        coming = lax.ppermute(block, axis, right) if turn < size - 1 else None
+        absorb = contribution(block, (mine - turn) % size * rows)
+        total = absorb if total is None else total + absorb
+        block = coming
+    return total
 
 
 def passed_along(block, axis, distance):
@@ -39,8 +51,17 @@
     mine = lax.dynamic_index_in_dim(features, lax.axis_index("ch"), 2, False)
     rows = lax.all_to_all(mine, "seq", 1, 0, tiled=True)
     rows = rows.reshape(n_seq * tok_rows, piece)
-    block = lax.all_gather(rows, "ch", axis=1, tiled=True)
-    partial = jnp.einsum("td,kdc->ktc", block, w_in, preferred_element_type=jnp.float32)
+    partial = summed_around(
+        rows,
+        "ch",
+        1,
+        lambda own_block, offset_2: jnp.einsum(
+            "td,kdc->ktc",
+            own_block,
+            lax.dynamic_slice_in_dim(w_in, offset_2, own_block.shape[1], axis=1),
+            preferred_element_type=jnp.float32,
+        ),
+    )
     return lax.psum_scatter(partial, "seq", scatter_dimension=1, tiled=True)
 
 

time: 416 us -> 472 us (1.13)
  matrix products: 32.8 us -> 95.2 us
  blocking collectives: 47.9 us -> 30.3 us
  waiting for transfers between devices: 288 us -> 271 us
  starting transfers between devices: 1.37 us -> 17.4 us
  local copies, waits for them, and re-layouts: 8.82 us -> 17.8 us
    dot_general x1 -> x8, matrix products: 18.9 us -> 81.3 us  [project(): jnp.einsum('td,kdc->ktc', own_block, lax.dynamic_slice_in_dim(w_in, offse...]
    all_gather x1 -> x0, waiting for transfers between devices: 37.4 us -> none  [project(): block = lax.all_gather(rows, 'ch', axis=1, tiled=True)]
    all_to_all x1 -> x0, blocking collectives: 17.5 us -> none  [project(): rows = lax.all_to_all(mine, 'seq', 1, 0, tiled=True)]
    all_to_all x0 -> x1, waiting for transfers between devices: none -> 12.5 us  [project(): rows = lax.all_to_all(mine, 'seq', 1, 0, tiled=True)]
    ppermute x0 -> x7, starting transfers between devices: none -> 11 us  [summed_around(): coming = lax.ppermute(block, axis, right) if turn < size - 1 else None]
    reduce_sum x0 -> x2, local copies, waits for them, and re-layouts: none -> 5.09 us  [the longest x1 2.55 us: per_device(): local = jnp.sum(falling * prefix, axis=1)]
    all_to_all x0 -> x1, starting transfers between devices: none -> 5.09 us  [project(): rows = lax.all_to_all(mine, 'seq', 1, 0, tiled=True)]
  transfers between devices with their start and end apart: 4 -> 11, of which waited for: 3 -> 8; matrix products, arithmetic and copies ran while one was open for 0% -> 10% of each run, Pallas kernels for 0% -> 0%
where the time goes in v1:
time: 472 us; the launch traced here: 471 us
  waiting for transfers between devices  271 us (57%)
  matrix products  95.2 us (20%)
  blocking collectives  30.3 us (6%)
  other arithmetic  25.1 us (5%)
  local copies, waits for them, and re-layouts  17.8 us (4%)
  starting transfers between devices  17.4 us (4%)
  between operations  13.6 us (3%)
    reduce_scatter x1, waiting for transfers between devices, project(): return lax.psum_scatter(partial, 'seq', scatter_dimension=1, tiled=True)  215 us
    dot_general x8, matrix products, project(): jnp.einsum('td,kdc->ktc', own_block, lax.dynamic_slice_in_dim(w_in, offse...  81.3 us
    all_gather x1, waiting for transfers between devices, project(): features = lax.all_gather(inputs, 'ch', axis=1, tiled=True)  39.5 us
    all_gather x2, blocking collectives, carried_in(): gathered = jax.tree.map(lambda a: lax.all_gather(a, axis), part)  30.3 us
    dot_general x1, matrix products, per_device(): jnp.dot(lower, rising.reshape(tok_rows, modes * width), precision=lax.Pre...  13.9 us
    all_to_all x1, waiting for transfers between devices, project(): rows = lax.all_to_all(mine, 'seq', 1, 0, tiled=True)  12.5 us
    ppermute x7, starting transfers between devices, summed_around(): coming = lax.ppermute(block, axis, right) if turn < size - 1 else None  11 us
  transfers between devices with their start and end apart: 11, of which 8 were waited for; matrix products, arithmetic and copies ran while one was open for 10% of the time, Pallas kernels for 0%

profile of v1, /device:TPU:26, one launch (start us, length us, event | category | flops | bytes accessed | tf_op | source)
XLA Modules:
  0.0 470.8 jit_solution(15886026251056045584)
XLA Ops:
  6.5 0.7 all-gather.4.cloned.1.call-update
  7.3 39.5 %all-gather.4.cloned.1.call-done = bf16[256,8192]{1,0:T(8,128)(2,1)} async-done(((bf16[256,1024]{1,0:T(8,128)(2,1)}), bf16[256,8192]{1,0:T(8,128)(2,1)}) %all-gather.4.cloned.1.call-update) | async-done | bytes 4194320 | tf_op jit(solution)/shard_map/all_gather | solution.py:48
  46.8 3.6 copy.58
  50.4 1.1 constant_dynamic-slice_fusion
  51.5 1.0 copy.64
  52.4 5.1 %all-to-all-start = ((bf16[256,4,256]{2,0,1:T(8,128)(2,1)}), bf16[256,4,256]{2,0,1:T(8,128)(2,1)S(1)}, u32[]{:S(2)}, u32[]{:S(2)}) async-start(bf16[256,4,256]{2,0,1:T(8,128)(2,1)} %bitcast.71), calls=%async_computation | async-start | bytes 1048576 | tf_op jit(solution)/shard_map/all_to_all | solution.py:52
  57.5 12.5 %all-to-all-done = bf16[256,4,256]{2,0,1:T(8,128)(2,1)S(1)} async-done(((bf16[256,4,256]{2,0,1:T(8,128)(2,1)}), bf16[256,4,256]{2,0,1:T(8,128)(2,1)S(1)}, u32[]{:S(2)}, u32[]{:S(2)}) %all-to-all-start) | async-done | bytes 524320 | tf_op jit(solution)/shard_map/all_to_all | solution.py:52
  70.1 0.0 collective-permute-start
  70.1 7.9 %fusion.15 = f32[3,1024,1024]{2,1,0:T(8,128)} fusion(bf16[1024,256,1]{1,0,2:T(8,128)(2,1)S(1)} %bitcast.83, bf16[3,2048,1024]{2,1,0:T(8,128)(2,1)} %param.9, s32[]{:T(128)S(6)} %select_n.70), kind=kOutput, calls=%fused_computation.26 | convolution fusion | flops 1610612736 | bytes 14680068 | tf_op jit(solution)/shard_map/td,kdc->ktc/dot_general | solution.py:58
  78.0 0.7 collective-permute-done
  78.7 0.7 collective-permute-start.1
  79.4 7.7 %fusion.13 = f32[3,1024,1024]{2,1,0:T(8,128)} fusion(bf16[3,2048,1024]{2,1,0:T(8,128)(2,1)} %param.9, s32[]{:T(128)S(6)} %select_n.73, bf16[1024,256]{1,0:T(8,128)(2,1)S(1)} %collective-permute-done), kind=kOutput, calls=%fused_computation.24 | convolution fusion | flops 1610612736 | bytes 14680068 | tf_op jit(solution)/shard_map/td,kdc->ktc/dot_general | solution.py:58
  87.1 0.2 collective-permute-done.1
  87.3 1.5 collective-permute-start.2
  88.7 0.0 slice-done
  88.7 0.0 slice-done.2
  88.8 6.3 %fusion.11 = f32[3,1024,1024]{2,1,0:T(8,128)} fusion(bf16[3,2048,1024]{2,1,0:T(8,128)(2,1)S(1)} %bitcast.79, s32[]{:T(128)S(6)} %select_n.75, bf16[1024,256]{1,0:T(8,128)(2,1)S(1)} %collective-permute-done.1), kind=kOutput, calls=%fused_computation.22 | convolution fusion | flops 1610612736 | bytes 14680068 | tf_op jit(solution)/shard_map/td,kdc->ktc/dot_general | solution.py:58
  95.1 0.8 collective-permute-done.2
  95.9 1.0 collective-permute-start.3
  96.9 6.5 %fusion.9 = f32[3,1024,1024]{2,1,0:T(8,128)} fusion(bf16[3,2048,1024]{2,1,0:T(8,128)(2,1)S(1)} %bitcast.79, s32[]{:T(128)S(6)} %select_n.77, bf16[1024,256]{1,0:T(8,128)(2,1)S(1)} %collective-permute-done.2), kind=kOutput, calls=%fused_computation.20 | convolution fusion | flops 1610612736 | bytes 14680068 | tf_op jit(solution)/shard_map/td,kdc->ktc/dot_general | solution.py:58
  103.3 1.2 collective-permute-done.3
  104.5 2.0 collective-permute-start.4
  106.5 6.3 %fusion.7 = f32[3,1024,1024]{2,1,0:T(8,128)} fusion(bf16[3,2048,1024]{2,1,0:T(8,128)(2,1)S(1)} %bitcast.79, s32[]{:T(128)S(6)} %select_n.79, bf16[1024,256]{1,0:T(8,128)(2,1)S(1)} %collective-permute-done.3), kind=kOutput, calls=%fused_computation.18 | convolution fusion | flops 1610612736 | bytes 14680068 | tf_op jit(solution)/shard_map/td,kdc->ktc/dot_general | solution.py:58
  112.8 0.3 collective-permute-done.4
  113.1 2.8 collective-permute-start.5
  115.9 6.4 %fusion.5 = f32[3,1024,1024]{2,1,0:T(8,128)} fusion(bf16[3,2048,1024]{2,1,0:T(8,128)(2,1)S(1)} %bitcast.79, s32[]{:T(128)S(6)} %select_n.81, bf16[1024,256]{1,0:T(8,128)(2,1)S(1)} %collective-permute-done.4), kind=kOutput, calls=%fused_computation.16 | convolution fusion | flops 1610612736 | bytes 14680068 | tf_op jit(solution)/shard_map/td,kdc->ktc/dot_general | solution.py:58
  122.3 0.0 collective-permute-done.5
  122.3 3.2 collective-permute-start.6
  125.4 6.4 %fusion.3 = f32[3,1024,1024]{2,1,0:T(8,128)} fusion(bf16[3,2048,1024]{2,1,0:T(8,128)(2,1)S(1)} %bitcast.79, s32[]{:T(128)S(6)} %select_n.83, bf16[1024,256]{1,0:T(8,128)(2,1)S(1)} %collective-permute-done.5), kind=kOutput, calls=%fused_computation.14 | convolution fusion | flops 1610612736 | bytes 14680068 | tf_op jit(solution)/shard_map/td,kdc->ktc/dot_general | solution.py:58
  131.8 0.0 collective-permute-done.6
  131.8 33.7 %add_bitcast_fusion = f32[3,1024,1024]{1,2,0:T(8,128)} fusion(f32[3,1024,1024]{2,1,0:T(8,128)} %fusion.3, f32[3,1024,1024]{2,1,0:T(8,128)} %fusion.5, f32[3,1024,1024]{2,1,0:T(8,128)} %fusion.7, f32[3,1024,1024]{2,1,0:T(8,128)} %fusion.9, f32[3,1024,1024]{2,1,0:T(8,128)} %fusion.11, f32[3,1024,1024]{2,1,0:T(8,128)} %fusion.15, f32[3,1024,1024]{2,1,0:T(8,128)} %fusion.13, ...), kind=kOutput, calls=%fused_computation.6 | convolution fusion | flops 1632632832 | bytes 102760448 | tf_op jit(solution)/shard_map/td,kdc->ktc/dot_general | solution.py:58
  165.5 0.0 reduce-scatter.2.cloned.1.call-update
  165.6 0.7 copy-done.3
  166.4 0.0 copy-done
  166.4 0.6 fusion.38
  167.0 215.2 %reduce-scatter.2.cloned.1.call-done = f32[3,256,1024]{1,2,0:T(8,128)} async-done(((f32[3,1024,1024]{1,2,0:T(8,128)}), f32[3,256,1024]{1,2,0:T(8,128)}) %reduce-scatter.2.cloned.1.call-update) | async-done | bytes 3145744 | tf_op jit(solution)/shard_map/reduce_scatter | solution.py:65
  382.2 2.0 convert_element_type.10
  384.3 0.3 slice.40
  384.5 0.3 copy.39
  384.8 1.3 collective-permute-start.7
  386.1 15.7 %all-gather = f32[64,1024]{1,0:T(8,128)S(1)} all-gather(f32[16,1024]{1,0:T(8,128)S(1)} %get-tuple-element.63), channel_id=2, replica_groups=mesh['seq'=4,'ch'=8] {'seq'}, dimensions={0}, use_global_device_ids=true | all-gather | bytes 327680 | tf_op jit(solution)/shard_map/all_gather | solution.py:29
  401.9 0.6 copy.59
  402.5 0.0 collective-permute-done.7
  402.5 0.4 copy.40
  403.0 1.0 maximum_convert_fusion
  403.9 3.2 fusion
  407.1 1.1 fusion.17
  408.2 2.5 copy.41
  410.8 4.1 multiply_reduce_fusion.1
  414.9 14.6 %all-gather.1 = f32[64,1024]{1,0:T(8,128)} all-gather(f32[16,1024]{1,0:T(8,128)S(1)} %multiply_reduce_fusion.1), channel_id=3, replica_groups=mesh['seq'=4,'ch'=8] {'seq'}, dimensions={0}, use_global_device_ids=true | all-gather | bytes 327680 | tf_op jit(solution)/shard_map/all_gather | solution.py:29
  429.5 2.9 while.12
  429.5 0.9 bitcast_add_fusion.2
  430.4 0.9 bitcast_add_fusion.2
  431.3 0.9 bitcast_add_fusion.2
  432.4 0.0 copy-start.1
  432.4 3.9 bitcast_multiply_fusion.1
  436.4 0.0 copy-done.1
  436.4 0.0 copy-start.4
  436.5 13.9 %multiply_reduce_fusion.2 = f32[256,1024]{1,0:T(8,128)} fusion(f32[16,1024,256]{2,1,0:T(8,128)S(1)} %bitcast.77, f32[16,1024]{1,0:T(8,128)S(1)} %get-tuple-element.61, f32[256]{0:T(256)S(1)} %iota_add_fusion.1, f32[16,1024]{1,0:T(8,128)S(1)} %copy-done.2), kind=kOutput, calls=%fused_computation.5 | convolution fusion | flops 12901482496 | bytes 17957888 | tf_op jit(solution)/shard_map/dot_general | solution.py:97
  450.4 2.6 copy.43
  453.0 3.8 multiply_reduce_fusion
  456.7 2.5 copy.44
  459.3 2.6 fusion.19
  461.9 2.0 copy.45
  (20 shorter events, 0.1 us)
Async XLA Ops:
  6.5 40.3 %all-gather.4.cloned.1.call-start = ((), (), s32[]{:S(2)}) async-start(), calls=%async_computation.2 | async-start | bytes 4718592 | tf_op jit(solution)/shard_map/all_gather | solution.py:48
  52.4 17.6 %all-to-all-start = ((bf16[256,4,256]{2,0,1:T(8,128)(2,1)}), bf16[256,4,256]{2,0,1:T(8,128)(2,1)S(1)}, u32[]{:S(2)}, u32[]{:S(2)}) async-start(bf16[256,4,256]{2,0,1:T(8,128)(2,1)} %bitcast.71), calls=%async_computation | async-start | bytes 1048576 | tf_op jit(solution)/shard_map/all_to_all | solution.py:52
  57.5 324.7 %reduce-scatter.2.cloned.1.call-start = ((), (), s32[]{:S(2)}) async-start(), calls=%async_computation.3 | async-start | bytes 15728640 | tf_op jit(solution)/shard_map/reduce_scatter | solution.py:65
  70.1 8.6 %collective-permute-start = (bf16[1024,256]{1,0:T(8,128)(2,1)S(1)}, bf16[1024,256]{1,0:T(8,128)(2,1)S(1)}, u32[]{:S(2)}, u32[]{:S(2)}) collective-permute-start(bf16[1024,256]{1,0:T(8,128)(2,1)S(1)} %bitcast.82), channel_id=1, source_target_pairs={{0,1},{1,2},{2,3},{3,4},{4,5},{5,6},{6,7},{7,0},{8,9},{9,10},{10,1... | collective-permute-start | bytes 1572872 | tf_op jit(solution)/shard_map/ppermute | solution.py:14
  70.1 18.7 %slice-start = ((s8[12582912]{0:T(1024)(128)(4,1)}), s8[4194304]{0:T(1024)(128)(4,1)S(1)}, s32[]{:S(2)}) async-start(s8[12582912]{0:T(1024)(128)(4,1)} %bitcast.78), calls=%async_computation.4 | async-start | bytes 8388608
  70.1 18.7 %slice-start.1 = ((s8[12582912]{0:T(1024)(128)(4,1)}), s8[4194304]{0:T(1024)(128)(4,1)S(1)}, s32[]{:S(2)}) async-start(s8[12582912]{0:T(1024)(128)(4,1)} %bitcast.78), calls=%async_computation.5 | async-start | bytes 8388608
  78.0 10.8 %slice-start.2 = ((s8[12582912]{0:T(1024)(128)(4,1)}), s8[4194304]{0:T(1024)(128)(4,1)S(1)}, s32[]{:S(2)}) async-start(s8[12582912]{0:T(1024)(128)(4,1)} %bitcast.78), calls=%async_computation.6 | async-start | bytes 8388608
  78.7 8.6 %collective-permute-start.1 = (bf16[1024,256]{1,0:T(8,128)(2,1)S(1)}, bf16[1024,256]{1,0:T(8,128)(2,1)S(1)}, u32[]{:S(2)}, u32[]{:S(2)}) collective-permute-start(bf16[1024,256]{1,0:T(8,128)(2,1)S(1)} %collective-permute-done), channel_id=1, source_target_pairs={{0,1},{1,2},{2,3},{3,4},{4,5},{5,6},{6,7},{7,0},{8,9},{9,10},{10,1... | collective-permute-start | bytes 1572872 | tf_op jit(solution)/shard_map/ppermute | solution.py:14
  87.3 8.6 %collective-permute-start.2 = (bf16[1024,256]{1,0:T(8,128)(2,1)S(1)}, bf16[1024,256]{1,0:T(8,128)(2,1)S(1)}, u32[]{:S(2)}, u32[]{:S(2)}) collective-permute-start(bf16[1024,256]{1,0:T(8,128)(2,1)S(1)} %collective-permute-done.1), channel_id=1, source_target_pairs={{0,1},{1,2},{2,3},{3,4},{4,5},{5,6},{6,7},{7,0},{8,9},{9,10},{10,1... | collective-permute-start | bytes 1572872 | tf_op jit(solution)/shard_map/ppermute | solution.py:14
  95.9 8.6 %collective-permute-start.3 = (bf16[1024,256]{1,0:T(8,128)(2,1)S(1)}, bf16[1024,256]{1,0:T(8,128)(2,1)S(1)}, u32[]{:S(2)}, u32[]{:S(2)}) collective-permute-start(bf16[1024,256]{1,0:T(8,128)(2,1)S(1)} %collective-permute-done.2), channel_id=1, source_target_pairs={{0,1},{1,2},{2,3},{3,4},{4,5},{5,6},{6,7},{7,0},{8,9},{9,10},{10,1... | collective-permute-start | bytes 1572872 | tf_op jit(solution)/shard_map/ppermute | solution.py:14
  104.5 8.6 %collective-permute-start.4 = (bf16[1024,256]{1,0:T(8,128)(2,1)S(1)}, bf16[1024,256]{1,0:T(8,128)(2,1)S(1)}, u32[]{:S(2)}, u32[]{:S(2)}) collective-permute-start(bf16[1024,256]{1,0:T(8,128)(2,1)S(1)} %collective-permute-done.3), channel_id=1, source_target_pairs={{0,1},{1,2},{2,3},{3,4},{4,5},{5,6},{6,7},{7,0},{8,9},{9,10},{10,1... | collective-permute-start | bytes 1572872 | tf_op jit(solution)/shard_map/ppermute | solution.py:14
  113.1 9.2 %collective-permute-start.5 = (bf16[1024,256]{1,0:T(8,128)(2,1)S(1)}, bf16[1024,256]{1,0:T(8,128)(2,1)S(1)}, u32[]{:S(2)}, u32[]{:S(2)}) collective-permute-start(bf16[1024,256]{1,0:T(8,128)(2,1)S(1)} %collective-permute-done.4), channel_id=1, source_target_pairs={{0,1},{1,2},{2,3},{3,4},{4,5},{5,6},{6,7},{7,0},{8,9},{9,10},{10,1... | collective-permute-start | bytes 1572872 | tf_op jit(solution)/shard_map/ppermute | solution.py:14
  122.3 9.6 %collective-permute-start.6 = (bf16[1024,256]{1,0:T(8,128)(2,1)S(1)}, bf16[1024,256]{1,0:T(8,128)(2,1)S(1)}, u32[]{:S(2)}, u32[]{:S(2)}) collective-permute-start(bf16[1024,256]{1,0:T(8,128)(2,1)S(1)} %collective-permute-done.5), channel_id=1, source_target_pairs={{0,1},{1,2},{2,3},{3,4},{4,5},{5,6},{6,7},{7,0},{8,9},{9,10},{10,1... | collective-permute-start | bytes 1572872 | tf_op jit(solution)/shard_map/ppermute | solution.py:14
  165.5 0.8 copy-start.3
  165.5 0.9 copy-start
  384.8 17.7 %collective-permute-start.7 = (bf16[3,2,1024]{2,1,0:T(2,128)(2,1)S(1)}, bf16[3,2,1024]{2,1,0:T(2,128)(2,1)S(1)}, u32[]{:S(2)}, u32[]{:S(2)}) collective-permute-start(bf16[3,2,1024]{2,1,0:T(2,128)(2,1)S(1)} %copy.39), channel_id=1, source_target_pairs={{0,8},{8,16},{16,24},{1,9},{9,17},{17,25},{2,10},{10,18},{18,26},{... | collective-permute-start | bytes 36872 | tf_op jit(solution)/shard_map/ppermute | solution.py:24
  432.4 4.0 copy-start.1
  432.4 4.0 copy-start.2
  436.4 22.8 %copy-start.4 = (f32[1024]{0:T(1024)S(1)}, f32[1024]{0:T(1024)}, u32[]{:S(2)}) copy-start(f32[1024]{0:T(1024)} %param.13) | copy-start | bytes 12292
Sparse Core Ops, SparseCore 0:
  9.2 37.5 all-gather.3
  165.7 216.5 reduce-scatter.1
